TPU v7x, 128 devices: a whole 4x4x4 slice. The times are simulated.
128 devices in a mesh: section: 2 (over core), seq: 64 (over z, x, y).
Axes of the slice: x: 4, y: 4, z: 4, core: 2. Of those that a mesh axis runs over, the one named last changes fastest.
Arguments:
- patches: bfloat16 [32768, 1408], P('seq'), may hold values from -42 to 42
- image_grid: int32 [256, 2], P('seq'), may hold values from 2 to 52, as said below
- image_offsets: int32 [256], P('seq'), may hold values from 0 to 32736, as said below
- dest_positions: int32 [8192], replicated, may hold values from 0 to 16383, as said below
- text_embeds: bfloat16 [256, 64, 1408], P(None, 'seq'), may hold values from -42 to 42
- segment_ids: int32 [256, 64], replicated, may hold values from 0 to 3, as said below
- vision_qkv: bfloat16 [1408, 3, 1408], P(None, None, 'section'), may hold values from -0.15625 to 0.15625
- vision_out: bfloat16 [1408, 1408], P('section'), may hold values from -0.875 to 0.875
- projector: bfloat16 [4, 1408, 1408], P('section'), may hold values from -0.078125 to 0.078125
- decoder_q: bfloat16 [1408, 1408], P(None, 'section'), may hold values from -0.15625 to 0.15625
- decoder_kv: bfloat16 [1408, 2, 176], P(None, None, 'section'), may hold values from -0.15625 to 0.15625
- decoder_out: bfloat16 [1408, 1408], P('section'), may hold values from -0.875 to 0.875
Outputs:
- decoded: bfloat16 [256, 64, 1408], P(None, 'seq')
Inputs may be any that keep to these rules, and one draw needn't show every extreme that they name: `image_grid`: patch rows and columns are even, columns are 8 or 16; the images of one index of seq lie back to back and cover exactly its 512 patches. `image_offsets`: each image's first patch; images are in order, back to back, the first of an index of seq at its first patch. `dest_positions`: the 128 merged rows of one index of seq go, in order, to 128 consecutive prompt positions; the ranges of different indices do not meet. `segment_ids`: never falls along prompt positions; every document number is used.
All inputs are finite; a program needn't handle non-finite values.
Results may differ from a plain program's by a relative error of at most 0.025.
Values may be sent and summed in bfloat16 or wider, within the bound.
No kernel may reach another device: no remote copies, remote signals or barrier semaphores. Data moves between devices by JAX's collectives and lax.ppermute only.
A program may use at most 128 MiB of HBM per device.

v0:
```python
import math
import jax
import jax.numpy as jnp
from jax import lax
from jax.sharding import PartitionSpec as P

D = 1408
HEAD = 88


def layer_norm(values):
    values = values.astype(jnp.float32)
    centred = values - jnp.mean(values, -1, keepdims=True)
    return centred * lax.rsqrt(jnp.mean(centred * centred, -1, keepdims=True) + 1e-06)


def root_norm(values):
    values = values.astype(jnp.float32)
    return values * lax.rsqrt(jnp.mean(values * values, -1, keepdims=True) + 1e-06)


def merge_rows(grid, offsets, count):
    heights = grid[:, 0]
    widths = grid[:, 1]
    group_start = offsets // 4
    group_count = heights * widths // 4
    merged_ids = jnp.arange(count, dtype=jnp.int32)
    inside = (
        (merged_ids[:, None] >= group_start[None, :])
        & (merged_ids[:, None] < (group_start + group_count)[None, :])
    ).astype(jnp.int32)
    first_group = jnp.sum(inside * group_start[None, :], 1)
    first_patch = jnp.sum(inside * offsets[None, :], 1)
    row_width = jnp.sum(inside * widths[None, :], 1)
    within = merged_ids - first_group
    groups_across = row_width // 2
    group_row = within // groups_across
    group_col = within % groups_across
    corner = first_patch + 2 * group_row * row_width + 2 * group_col
    return jnp.stack([corner, corner + 1, corner + row_width, corner + row_width + 1], 1)


def body(
    patches,
    image_grid,
    image_offsets,
    dest_positions,
    text_embeds,
    segment_ids,
    vision_qkv,
    vision_out,
    projector,
    decoder_q,
    decoder_kv,
    decoder_out,
):
    section_index = lax.axis_index("section")
    seq_index = lax.axis_index("seq")
    seq_count = lax.axis_size("seq")
    scale = 3.0 / math.sqrt(HEAD)
    patch_count = patches.shape[0]
    local_heads = vision_out.shape[0] // HEAD
    merged_count = patch_count // 4
    normed = layer_norm(patches).astype(jnp.bfloat16)
    mixed = jnp.dot(normed, vision_qkv.reshape(D, -1), preferred_element_type=jnp.float32).reshape(
        patch_count, 3, local_heads, HEAD
    )
    queries = root_norm(mixed[:, 0]).astype(jnp.bfloat16)
    keys = root_norm(mixed[:, 1]).astype(jnp.bfloat16)
    values = mixed[:, 2].astype(jnp.bfloat16)
    offsets = image_offsets - seq_index * patch_count
    image_of = jnp.sum(
        (jnp.arange(patch_count, dtype=jnp.int32)[:, None] >= offsets[None, :]).astype(jnp.int32), 1
    )
    query_block = math.gcd(patch_count, 512)

    def vision_block(first):
        scores = (
            jnp.einsum("qhd,khd->hqk", queries, keys, preferred_element_type=jnp.float32) * scale
        )
        same = (image_of[:, None] == image_of[None, :])[None]
        weights = jnp.where(same, jnp.exp(scores), jnp.zeros_like(scores))
        totals = jnp.sum(weights, -1)
        mixed_values = jnp.einsum(
            "hqk,khd->qhd", weights.astype(jnp.bfloat16), values, preferred_element_type=jnp.float32
        )
        return (
            (mixed_values / jnp.transpose(totals)[:, :, None])
            .astype(jnp.bfloat16)
            .reshape(query_block, local_heads * HEAD)
        )

    attended = lax.map(
        vision_block, jnp.arange(patch_count // query_block, dtype=jnp.int32) * query_block
    )
    attended = attended.reshape(patch_count, local_heads * HEAD)
    picks = merge_rows(image_grid, offsets, merged_count)
    own_picks = lax.dynamic_slice_in_dim(picks, 2 * section_index, 2, 1).reshape(-1)
    head_terms = jnp.dot(attended, vision_out, preferred_element_type=jnp.float32)
    vision = (patches.astype(jnp.float32) + lax.psum(head_terms, "section")).astype(jnp.bfloat16)
    kept = vision[own_picks]
    merge_terms = jnp.dot(
        kept.reshape(merged_count, 2 * D),
        projector.reshape(2 * D, D),
        preferred_element_type=jnp.float32,
    )
    per_peer = merged_count // seq_count
    run_starts = dest_positions.reshape(seq_count, merged_count)[:, 0]
    own_start = run_starts[seq_index]
    image_rows = lax.psum(merge_terms, "section").astype(jnp.bfloat16)
    received = lax.all_to_all(
        jnp.roll(image_rows.reshape(per_peer, seq_count, image_rows.shape[1]), own_start, axis=1),
        "seq",
        split_axis=1,
        concat_axis=1,
        tiled=True,
    )
    slot_base = jnp.arange(per_peer, dtype=jnp.int32)[:, None] * seq_count
    landing = (
        run_starts[None, :] + slot_base + (seq_index - run_starts[None, :]) % seq_count
    ) // seq_count
    text_rows = text_embeds.shape[0]
    prompt = text_embeds.reshape(text_rows, D).at[landing.reshape(-1)].set(received.reshape(-1, D))
    text_normed = root_norm(prompt).astype(jnp.bfloat16)
    kv_local = decoder_kv.shape[2] // HEAD
    group = local_heads // kv_local
    text_queries = root_norm(
        jnp.dot(text_normed, decoder_q, preferred_element_type=jnp.float32).reshape(
            text_rows, local_heads, HEAD
        )
    )
    text_queries = text_queries.astype(jnp.bfloat16).reshape(text_rows, kv_local, group, HEAD)
    paired = jnp.dot(
        text_normed, decoder_kv.reshape(D, -1), preferred_element_type=jnp.float32
    ).reshape(text_rows, 2, kv_local, HEAD)
    key_rows = root_norm(paired[:, 0]).astype(jnp.bfloat16)
    value_rows = paired[:, 1].astype(jnp.bfloat16)
    shared = jnp.stack([key_rows, value_rows], 1)[None]
    query_places = jnp.arange(text_rows, dtype=jnp.int32) * seq_count + seq_index
    query_segments = lax.dynamic_slice_in_dim(segment_ids, seq_index, 1, 1)[:, 0]
    start_state = (
        jnp.zeros((text_rows, kv_local, group, HEAD), jnp.float32),
        jnp.zeros((text_rows, kv_local, group), jnp.float32),
    )
    piece = lax.all_gather(shared, "seq", axis=0, tiled=True)
    shards = piece.shape[0]
    stride = math.gcd(shards, 8)
    blocks = shards // stride
    key_segments = jnp.transpose(segment_ids).reshape(blocks, stride * text_rows)
    shard_ids = jnp.arange(shards, dtype=jnp.int32)
    key_places = (
        jnp.arange(text_rows, dtype=jnp.int32)[None, :] * seq_count + shard_ids[:, None]
    ).reshape(blocks, stride * text_rows)
    grouped = piece.reshape(blocks, stride * text_rows, 2, kv_local, HEAD)

    def one_block(state, inputs):
        block_pair, block_places, block_segments = inputs
        scores = (
            jnp.einsum(
                "qkgd,lkd->qkgl", text_queries, block_pair[:, 0], preferred_element_type=jnp.float32
            )
            * scale
        )
        allowed = (block_places[None, :] <= query_places[:, None]) & (
            block_segments[None, :] == query_segments[:, None]
        )
        weights = jnp.where(allowed[:, None, None, :], jnp.exp(scores), jnp.zeros_like(scores))
        totals = state[1] + jnp.sum(weights, -1)
        sums = state[0] + jnp.einsum(
            "qkgl,lkd->qkgd",
            weights.astype(jnp.bfloat16),
            block_pair[:, 1],
            preferred_element_type=jnp.float32,
        )
        return ((sums, totals), None)

    result, unused = lax.scan(one_block, start_state, (grouped, key_places, key_segments))
    sums, totals = result
    attended_text = (
        (sums / totals[..., None]).astype(jnp.bfloat16).reshape(text_rows, local_heads * HEAD)
    )
    output_terms = jnp.dot(attended_text, decoder_out, preferred_element_type=jnp.float32)
    decoded = (prompt.astype(jnp.float32) + lax.psum(output_terms, "section")).astype(jnp.bfloat16)
    return decoded.reshape(text_rows, 1, D)


def solution(mesh):
    placed = (
        P("seq", None),
        P("seq", None),
        P("seq"),
        P(),
        P(None, "seq", None),
        P(),
        P(None, None, "section"),
        P("section", None),
        P("section", None, None),
        P(None, "section"),
        P(None, None, "section"),
        P("section", None),
    )
    return jax.shard_map(
        body, mesh=mesh, in_specs=placed, out_specs=P(None, "seq", None), check_vma=False
    )
```

profile of v0, /device:TPU:1, one launch (start us, length us, event | category | flops | bytes accessed | tf_op | source)
XLA Modules:
  0.0 298.4 jit_solution(1817690820470734248)
XLA Ops:
  9.9 6.0 %fusion.37 = f32[512,3,8,88]{0,3,2,1:T(8,128)S(1)} fusion(bf16[3,8,88,1408]{3,2,1,0:T(8,128)(2,1)} %bitcast.211, bf16[512,1408]{1,0:T(8,128)(2,1)S(1)} %copy-done.3, f32[512]{0:T(512)S(1)} %add_rsqrt_fusion.3, f32[512]{0:T(512)S(1)} %broadcast_multiply_fusion), kind=kOutput, calls=%fused_computation.47 | convolution fusion | flops 3047948288 | bytes 11718656 | tf_op jit(solution)/shard_map/dot_general | solution.py:65
  16.4 2.5 fusion.18
  20.7 3.1 %fusion.66 = f32[512,1408]{1,0:T(8,128)} fusion(bf16[512,704]{0,1:T(8,128)(2,1)S(1)} %bitcast.203, bf16[704,1408]{1,0:T(8,128)(2,1)S(1)} %copy-done), kind=kOutput, calls=%fused_computation.146 | convolution fusion | flops 1015021568 | bytes 5586944 | tf_op jit(solution)/shard_map/dot_general | solution.py:99
  27.0 28.8 %all-reduce.4.cloned.1.call-done = f32[512,1408]{1,0:T(8,128)} async-done(((f32[512,1408]{1,0:T(8,128)}), f32[512,1408]{1,0:T(8,128)}) %all-reduce.4.cloned.1.call-update) | async-done | bytes 2883600 | tf_op jit(solution)/shard_map/psum | solution.py:100
  55.8 2.1 fusion.29
  59.5 4.5 %fusion.67 = f32[128,1408]{1,0:T(8,128)S(1)} fusion(bf16[128,2816]{1,0:T(8,128)(2,1)S(1)} %reshape.607, bf16[2816,1408]{1,0:T(8,128)(2,1)} %bitcast.193), kind=kOutput, calls=%fused_computation.147 | convolution fusion | flops 1015021568 | bytes 9371648 | tf_op jit(solution)/shard_map/dot_general | solution.py:102
  64.0 5.7 %all-reduce.7 = bf16[128,1408]{1,0:T(8,128)(2,1)S(1)} all-reduce(f32[128,1408]{1,0:T(8,128)S(1)} %fusion.67), channel_id=1, replica_groups=mesh['section'=2,'seq'=64] {'section'}, use_global_device_ids=true, to_apply=%region_10.11 | all-reduce | flops 180224 | bytes 1081344 | tf_op jit(solution)/shard_map/psum | solution.py:110
  71.8 10.1 %all-to-all-start = ((bf16[2,64,1408]{2,0,1:T(2,128)(2,1)}), bf16[2,64,1408]{2,0,1:T(2,128)(2,1)S(1)}, u32[]{:S(2)}, u32[]{:S(2)}) async-start(bf16[2,64,1408]{2,0,1:T(2,128)(2,1)} %fusion.51), calls=%async_computation | async-start | bytes 720896 | tf_op jit(solution)/shard_map/all_to_all | solution.py:111
  82.1 10.5 %all-to-all-done = bf16[2,64,1408]{2,0,1:T(2,128)(2,1)S(1)} async-done(((bf16[2,64,1408]{2,0,1:T(2,128)(2,1)}), bf16[2,64,1408]{2,0,1:T(2,128)(2,1)S(1)}, u32[]{:S(2)}, u32[]{:S(2)}) %all-to-all-start) | async-done | bytes 360480 | tf_op jit(solution)/shard_map/all_to_all | solution.py:111
  96.0 2.4 fusion.65
  98.5 76.8 %all-gather.3.cloned.1.call-done = bf16[16384,2,1,88]{0,3,1,2:T(8,128)(2,1)} async-done(((bf16[256,2,1,88]{0,3,1,2:T(8,128)(2,1)}), bf16[16384,2,1,88]{0,3,1,2:T(8,128)(2,1)}) %all-gather.3.cloned.1.call-update) | async-done | bytes 5767184 | tf_op jit(solution)/shard_map/all_gather | solution.py:145
  175.3 6.1 %copy.44 = bf16[1,2,11,8,8,2048]{5,4,2,1,0,3:T(8,128)(2,1)} copy(bf16[1,2,11,8,8,2048]{5,4,3,2,1,0:T(8,128)(2,1)} %bitcast.195) | data formatting | bytes 11534336 | tf_op jit(solution)/shard_map/reshape | solution.py:154
  181.4 76.3 %while.4 = (s32[]{:T(128)}, f32[256,1,8,88]{0,3,2,1:T(8,128)S(1)}, f32[256,1,8]{0,2,1:T(8,128)S(1)}, bf16[8,2048,2,1,88]{1,4,2,3,0:T(8,128)(2,1)}, s32[8,2048]{1...) while((s32[]{:T(128)}, f32[256,1,8,88]{0,3,2,1:T(8,128)S(1)}, ...), condition=%wide.region_17.18_spmd.clone, body=%wide.region_15.17_spmd.clone.sunk | while | flops 1503496704 | bytes 39177352 | solution.py:177
  184.1 3.9 %fusion.81 = (f32[256,8]{0,1:T(8,128)S(1)}, f32[2048,256,8]{1,0,2:T(8,128)S(1)}) fusion(pred[256,2048]{0,1:T(8,128)(4,1)S(1)} %compare_and_fusion.2, bf16[256,1,8,88]{0,3,2,1:T(8,128)(2,1)S(1)} %get-tuple-element.285, bf16[2048,2,1,88]{0,3,2,1:T(8,128)(2,1)S(1)} %dynamic-slice_bitcast_fusion.2), kind=kOutput, calls=%fused_computation.4.clone.1 | convolution fusion | flops 750778368 | bytes 18030592 | tf_op jit(solution)/shard_map/while/body/eval_jaxpr/qkgd,lkd->qkgl/dot_general | solution.py:159
  188.0 2.9 fusion.82
  193.7 3.9 %fusion.81 = (f32[256,8]{0,1:T(8,128)S(1)}, f32[2048,256,8]{1,0,2:T(8,128)S(1)}) fusion(pred[256,2048]{0,1:T(8,128)(4,1)S(1)} %compare_and_fusion.2, bf16[256,1,8,88]{0,3,2,1:T(8,128)(2,1)S(1)} %get-tuple-element.285, bf16[2048,2,1,88]{0,3,2,1:T(8,128)(2,1)S(1)} %dynamic-slice_bitcast_fusion.2), kind=kOutput, calls=%fused_computation.4.clone.1 | convolution fusion | flops 750778368 | bytes 18030592 | tf_op jit(solution)/shard_map/while/body/eval_jaxpr/qkgd,lkd->qkgl/dot_general | solution.py:159
  197.6 2.9 fusion.82
  203.2 3.9 %fusion.81 = (f32[256,8]{0,1:T(8,128)S(1)}, f32[2048,256,8]{1,0,2:T(8,128)S(1)}) fusion(pred[256,2048]{0,1:T(8,128)(4,1)S(1)} %compare_and_fusion.2, bf16[256,1,8,88]{0,3,2,1:T(8,128)(2,1)S(1)} %get-tuple-element.285, bf16[2048,2,1,88]{0,3,2,1:T(8,128)(2,1)S(1)} %dynamic-slice_bitcast_fusion.2), kind=kOutput, calls=%fused_computation.4.clone.1 | convolution fusion | flops 750778368 | bytes 18030592 | tf_op jit(solution)/shard_map/while/body/eval_jaxpr/qkgd,lkd->qkgl/dot_general | solution.py:159
  207.1 2.9 fusion.82
  212.8 3.9 %fusion.81 = (f32[256,8]{0,1:T(8,128)S(1)}, f32[2048,256,8]{1,0,2:T(8,128)S(1)}) fusion(pred[256,2048]{0,1:T(8,128)(4,1)S(1)} %compare_and_fusion.2, bf16[256,1,8,88]{0,3,2,1:T(8,128)(2,1)S(1)} %get-tuple-element.285, bf16[2048,2,1,88]{0,3,2,1:T(8,128)(2,1)S(1)} %dynamic-slice_bitcast_fusion.2), kind=kOutput, calls=%fused_computation.4.clone.1 | convolution fusion | flops 750778368 | bytes 18030592 | tf_op jit(solution)/shard_map/while/body/eval_jaxpr/qkgd,lkd->qkgl/dot_general | solution.py:159
  216.6 2.9 fusion.82
  222.3 3.9 %fusion.81 = (f32[256,8]{0,1:T(8,128)S(1)}, f32[2048,256,8]{1,0,2:T(8,128)S(1)}) fusion(pred[256,2048]{0,1:T(8,128)(4,1)S(1)} %compare_and_fusion.2, bf16[256,1,8,88]{0,3,2,1:T(8,128)(2,1)S(1)} %get-tuple-element.285, bf16[2048,2,1,88]{0,3,2,1:T(8,128)(2,1)S(1)} %dynamic-slice_bitcast_fusion.2), kind=kOutput, calls=%fused_computation.4.clone.1 | convolution fusion | flops 750778368 | bytes 18030592 | tf_op jit(solution)/shard_map/while/body/eval_jaxpr/qkgd,lkd->qkgl/dot_general | solution.py:159
  226.2 2.9 fusion.82
  231.9 3.9 %fusion.81 = (f32[256,8]{0,1:T(8,128)S(1)}, f32[2048,256,8]{1,0,2:T(8,128)S(1)}) fusion(pred[256,2048]{0,1:T(8,128)(4,1)S(1)} %compare_and_fusion.2, bf16[256,1,8,88]{0,3,2,1:T(8,128)(2,1)S(1)} %get-tuple-element.285, bf16[2048,2,1,88]{0,3,2,1:T(8,128)(2,1)S(1)} %dynamic-slice_bitcast_fusion.2), kind=kOutput, calls=%fused_computation.4.clone.1 | convolution fusion | flops 750778368 | bytes 18030592 | tf_op jit(solution)/shard_map/while/body/eval_jaxpr/qkgd,lkd->qkgl/dot_general | solution.py:159
  235.7 2.9 fusion.82
  241.4 3.9 %fusion.81 = (f32[256,8]{0,1:T(8,128)S(1)}, f32[2048,256,8]{1,0,2:T(8,128)S(1)}) fusion(pred[256,2048]{0,1:T(8,128)(4,1)S(1)} %compare_and_fusion.2, bf16[256,1,8,88]{0,3,2,1:T(8,128)(2,1)S(1)} %get-tuple-element.285, bf16[2048,2,1,88]{0,3,2,1:T(8,128)(2,1)S(1)} %dynamic-slice_bitcast_fusion.2), kind=kOutput, calls=%fused_computation.4.clone.1 | convolution fusion | flops 750778368 | bytes 18030592 | tf_op jit(solution)/shard_map/while/body/eval_jaxpr/qkgd,lkd->qkgl/dot_general | solution.py:159
  245.3 2.9 fusion.82
  251.0 3.9 %fusion.81 = (f32[256,8]{0,1:T(8,128)S(1)}, f32[2048,256,8]{1,0,2:T(8,128)S(1)}) fusion(pred[256,2048]{0,1:T(8,128)(4,1)S(1)} %compare_and_fusion.2, bf16[256,1,8,88]{0,3,2,1:T(8,128)(2,1)S(1)} %get-tuple-element.285, bf16[2048,2,1,88]{0,3,2,1:T(8,128)(2,1)S(1)} %dynamic-slice_bitcast_fusion.2), kind=kOutput, calls=%fused_computation.4.clone.1 | convolution fusion | flops 750778368 | bytes 18030592 | tf_op jit(solution)/shard_map/while/body/eval_jaxpr/qkgd,lkd->qkgl/dot_general | solution.py:159
  254.8 2.9 fusion.82
  257.9 3.6 %fusion.68 = f32[256,1408]{1,0:T(8,128)} fusion(bf16[256,704]{0,1:T(8,128)(2,1)S(1)} %bitcast.200, bf16[704,1408]{1,0:T(8,128)(2,1)} %param.25), kind=kOutput, calls=%fused_computation.148 | convolution fusion | flops 507510784 | bytes 3784704 | tf_op jit(solution)/shard_map/dot_general | solution.py:182
  261.5 28.1 %all-reduce.6.cloned.1.call-done = f32[256,1408]{1,0:T(8,128)} async-done(((f32[256,1408]{1,0:T(8,128)}), f32[256,1408]{1,0:T(8,128)}) %all-reduce.6.cloned.1.call-update) | async-done | bytes 1441808 | tf_op jit(solution)/shard_map/psum | solution.py:183
  289.6 2.3 fusion.46
  (117 shorter events, 35.2 us)
Async XLA Ops:
  6.5 14.2 %copy-start = (bf16[704,1408]{1,0:T(8,128)(2,1)S(1)}, bf16[704,1408]{1,0:T(8,128)(2,1)}, u32[]{:S(2)}) copy-start(bf16[704,1408]{1,0:T(8,128)(2,1)} %param.21) | copy-start | bytes 5947396
  6.5 2.6 copy-start.3
  6.5 49.3 %all-reduce.4.cloned.1.call-start = ((), (), s32[]{:S(2)}) async-start(), calls=%async_computation.1 | async-start | bytes 5767168 | tf_op jit(solution)/shard_map/psum | solution.py:100
  20.7 3.1 %copy-start.5 = (s32[8192]{0:T(1024)S(1)}, s32[8192]{0:T(1024)}, u32[]{:S(2)}) copy-start(s32[8192]{0:T(1024)} %param.17) | copy-start | bytes 98308
  23.8 2.6 copy-start.6
  64.0 28.6 %copy-start.2 = (bf16[256,1,1408]{2,0,1:T(8,128)(2,1)S(1)}, bf16[256,1,1408]{2,0,1:T(8,128)(2,1)}, u32[]{:S(2)}) copy-start(bf16[256,1,1408]{2,0,1:T(8,128)(2,1)} %param.18) | copy-start | bytes 2162692
  71.8 20.8 %all-to-all-start = ((bf16[2,64,1408]{2,0,1:T(2,128)(2,1)}), bf16[2,64,1408]{2,0,1:T(2,128)(2,1)S(1)}, u32[]{:S(2)}, u32[]{:S(2)}) async-start(bf16[2,64,1408]{2,0,1:T(2,128)(2,1)} %fusion.51), calls=%async_computation | async-start | bytes 720896 | tf_op jit(solution)/shard_map/all_to_all | solution.py:111
  81.9 93.4 %all-gather.3.cloned.1.call-start = ((), (), s32[]{:S(2)}) async-start(), calls=%async_computation.3 | async-start | bytes 5857280 | tf_op jit(solution)/shard_map/all_gather | solution.py:145
  92.6 1.8 copy-start.7
  94.2 1.6 copy-start.4
  95.7 193.8 %all-reduce.6.cloned.1.call-start = ((), (), s32[]{:S(2)}) async-start(), calls=%async_computation.2 | async-start | bytes 2883584 | tf_op jit(solution)/shard_map/psum | solution.py:183
  257.9 34.0 %copy-start.1 = (bf16[704,1408]{1,0:T(8,128)(2,1)S(1)}, bf16[704,1408]{1,0:T(8,128)(2,1)}, u32[]{:S(2)}) copy-start(bf16[704,1408]{1,0:T(8,128)(2,1)} %param.21) | copy-start | bytes 5947396
Sparse Core Ops, SparseCore 0:
  23.9 31.8 all-reduce.3
  95.8 79.4 all-gather.2
  261.6 27.8 all-reduce.5
where the time goes:
time: 299 us; the launch traced here: 298 us
  waiting for transfers between devices  144 us (48%)
  matrix products  79 us (26%)
  other arithmetic  23 us (8%)
  local copies, waits for them, and re-layouts  20.3 us (7%)
  between operations  15.5 us (5%)
  starting transfers between devices  10.2 us (3%)
  blocking collectives  5.69 us (2%)
    all_gather x1, waiting for transfers between devices, body(): piece = lax.all_gather(shared, 'seq', axis=0, tiled=True)  76.8 us
    dot_general x8, matrix products, one_block(): jnp.einsum('qkgd,lkd->qkgl', text_queries, block_pair[:, 0], preferred_el...  31.2 us
    psum x1, waiting for transfers between devices, body(): lax.psum(head_terms, 'section')  28.8 us
    psum x1, waiting for transfers between devices, body(): lax.psum(output_terms, 'section')  28.1 us
    dot_general x8, matrix products, one_block(): jnp.einsum('qkgl,lkd->qkgd', weights.astype(jnp.bfloat16), block_pair[:,...  23.4 us
    and x8, other arithmetic, one_block(): (block_places[None, :] <= query_places[:, None]) & (block_segments[None,...  11.6 us
    all_to_all x1, waiting for transfers between devices, body(): lax.all_to_all(jnp.roll(image_rows.reshape(per_peer, seq_count, image_row...  10.5 us
    all_to_all x1, starting transfers between devices, body(): lax.all_to_all(jnp.roll(image_rows.reshape(per_peer, seq_count, image_row...  10.1 us
  transfers between devices with their start and end apart: 4, of which 4 were waited for; matrix products, arithmetic and copies ran while one was open for 1% of the time, Pallas kernels for 0%

commit v1 on v0

--- a/solution.py
+++ b/solution.py
@@ -142,7 +142,8 @@
         jnp.zeros((text_rows, kv_local, group, HEAD), jnp.float32),
         jnp.zeros((text_rows, kv_local, group), jnp.float32),
     )
-    piece = lax.all_gather(shared, "seq", axis=0, tiled=True)
+    repeated = jnp.stack([shared] * lax.axis_size("seq"))
+    piece = jnp.concatenate(lax.all_to_all(repeated, "seq", 0, 0), axis=0)
     shards = piece.shape[0]
     stride = math.gcd(shards, 8)
     blocks = shards // stride

time: 299 us -> 319 us (1.067)
  local copies, waits for them, and re-layouts: 20.3 us -> 42.5 us
  waiting for transfers between devices: 144 us -> 136 us
  starting transfers between devices: 10.2 us -> 16 us
    all_gather x1 -> x0, waiting for transfers between devices: 76.8 us -> none  [body(): piece = lax.all_gather(shared, 'seq', axis=0, tiled=True)]
    all_to_all x0 -> x1, waiting for transfers between devices: none -> 68.9 us  [body(): piece = jnp.concatenate(lax.all_to_all(repeated, 'seq', 0, 0), axis=0)]
    another operation x0 -> x2, local copies, waits for them, and re-layouts: none -> 12.7 us  [the longest x1 9.8 us: body(): grouped = piece.reshape(blocks, stride * text_rows, 2, kv_local, HEAD)]
    unnamed x18 -> x19, local copies, waits for them, and re-layouts: 0.05 us -> 8.32 us
    all_to_all x0 -> x1, local copies, waits for them, and re-layouts: none -> 7.27 us  [body(): piece = jnp.concatenate(lax.all_to_all(repeated, 'seq', 0, 0), axis=0)]
    reshape x1 -> x0, local copies, waits for them, and re-layouts: 6.1 us -> none  [body(): grouped = piece.reshape(blocks, stride * text_rows, 2, kv_local, HEAD)]
    all_to_all x0 -> x1, starting transfers between devices: none -> 5.82 us  [body(): piece = jnp.concatenate(lax.all_to_all(repeated, 'seq', 0, 0), axis=0)]
where the time goes in v1:
time: 319 us; the launch traced here: 318 us
  waiting for transfers between devices  136 us (43%)
  matrix products  79 us (25%)
  local copies, waits for them, and re-layouts  42.5 us (13%)
  other arithmetic  22.4 us (7%)
  starting transfers between devices  16 us (5%)
  between operations  15.8 us (5%)
  blocking collectives  5.69 us (2%)
    all_to_all x1, waiting for transfers between devices, body(): piece = jnp.concatenate(lax.all_to_all(repeated, 'seq', 0, 0), axis=0)  68.9 us
    dot_general x8, matrix products, one_block(): jnp.einsum('qkgd,lkd->qkgl', text_queries, block_pair[:, 0], preferred_el...  31.2 us
    psum x1, waiting for transfers between devices, body(): lax.psum(head_terms, 'section')  28.8 us
    psum x1, waiting for transfers between devices, body(): lax.psum(output_terms, 'section')  27.8 us
    dot_general x8, matrix products, one_block(): jnp.einsum('qkgl,lkd->qkgd', weights.astype(jnp.bfloat16), block_pair[:,...  23.4 us
    and x8, other arithmetic, one_block(): (block_places[None, :] <= query_places[:, None]) & (block_segments[None,...  11.6 us
    all_to_all x1, waiting for transfers between devices, body(): lax.all_to_all(jnp.roll(image_rows.reshape(per_peer, seq_count, image_row...  10.5 us
    all_to_all x1, starting transfers between devices, body(): lax.all_to_all(jnp.roll(image_rows.reshape(per_peer, seq_count, image_row...  10.1 us
  transfers between devices with their start and end apart: 4, of which 4 were waited for; matrix products, arithmetic and copies ran while one was open for 1% of the time, Pallas kernels for 0%

profile of v1, /device:TPU:1, one launch (start us, length us, event | category | flops | bytes accessed | tf_op | source)
XLA Modules:
  0.0 317.9 jit_solution(9741131239717566231)
XLA Ops:
  9.9 6.0 %fusion.37 = f32[512,3,8,88]{0,3,2,1:T(8,128)S(1)} fusion(bf16[3,8,88,1408]{3,2,1,0:T(8,128)(2,1)} %bitcast.211, bf16[512,1408]{1,0:T(8,128)(2,1)S(1)} %copy-done.3, f32[512]{0:T(512)S(1)} %add_rsqrt_fusion.3, f32[512]{0:T(512)S(1)} %broadcast_multiply_fusion), kind=kOutput, calls=%fused_computation.46 | convolution fusion | flops 3047948288 | bytes 11718656 | tf_op jit(solution)/shard_map/dot_general | solution.py:65
  20.7 3.1 fusion.66
  27.0 28.8 %all-reduce.4.cloned.1.call-done = f32[512,1408]{1,0:T(8,128)} async-done(((f32[512,1408]{1,0:T(8,128)}), f32[512,1408]{1,0:T(8,128)}) %all-reduce.4.cloned.1.call-update) | async-done | bytes 2883600 | tf_op jit(solution)/shard_map/psum | solution.py:100
  59.5 4.5 %fusion.67 = f32[128,1408]{1,0:T(8,128)S(1)} fusion(bf16[128,2816]{1,0:T(8,128)(2,1)S(1)} %reshape.607, bf16[2816,1408]{1,0:T(8,128)(2,1)} %bitcast.195), kind=kOutput, calls=%fused_computation.146 | convolution fusion | flops 1015021568 | bytes 9371648 | tf_op jit(solution)/shard_map/dot_general | solution.py:102
  64.0 5.7 %all-reduce.7 = bf16[128,1408]{1,0:T(8,128)(2,1)S(1)} all-reduce(f32[128,1408]{1,0:T(8,128)S(1)} %fusion.67), channel_id=1, replica_groups=mesh['section'=2,'seq'=64] {'section'}, use_global_device_ids=true, to_apply=%region_10.11 | all-reduce | flops 180224 | bytes 1081344 | tf_op jit(solution)/shard_map/psum | solution.py:110
  71.8 10.1 %all-to-all-start = ((bf16[2,64,1408]{2,0,1:T(2,128)(2,1)}), bf16[2,64,1408]{2,0,1:T(2,128)(2,1)S(1)}, u32[]{:S(2)}, u32[]{:S(2)}) async-start(bf16[2,64,1408]{2,0,1:T(2,128)(2,1)} %fusion.51), calls=%async_computation | async-start | bytes 720896 | tf_op jit(solution)/shard_map/all_to_all | solution.py:111
  82.1 10.5 %all-to-all-done = bf16[2,64,1408]{2,0,1:T(2,128)(2,1)S(1)} async-done(((bf16[2,64,1408]{2,0,1:T(2,128)(2,1)}), bf16[2,64,1408]{2,0,1:T(2,128)(2,1)S(1)}, u32[]{:S(2)}, u32[]{:S(2)}) %all-to-all-start) | async-done | bytes 360480 | tf_op jit(solution)/shard_map/all_to_all | solution.py:111
  95.1 2.9 stack.20
  98.0 5.8 %all-to-all-start.1 = ((bf16[64,1,256,2,1,88]{2,5,3,4,1,0:T(8,128)(2,1)}), bf16[64,1,256,2,1,88]{2,5,3,4,1,0:T(8,128)(2,1)}, u32[]{:S(2)}, u32[]{:S(2)}) async-start(bf16[64,1,256,2,1,88]{2,5,3,4,1,0:T(8,128)(2,1)} %stack.20), calls=%async_computation.1 | async-start | bytes 11534336 | tf_op jit(solution)/shard_map/all_to_all | solution.py:146
  106.6 68.9 %all-to-all-done.1 = bf16[64,1,256,2,1,88]{2,5,3,4,1,0:T(8,128)(2,1)} async-done(((bf16[64,1,256,2,1,88]{2,5,3,4,1,0:T(8,128)(2,1)}), bf16[64,1,256,2,1,88]{2,5,3,4,1,0:T(8,128)(2,1)}, u32[]{:S(2)}, u32[]{:S(2)}) %all-to-all-start.1) | async-done | bytes 5767200 | tf_op jit(solution)/shard_map/all_to_all | solution.py:146
  175.5 7.3 %copy.38 = bf16[64,1,256,2,1,88]{2,0,5,3,4,1:T(8,128)(2,1)} copy(bf16[64,1,256,2,1,88]{2,5,3,4,1,0:T(8,128)(2,1)} %all-to-all-done.1) | data formatting | bytes 11534336 | tf_op jit(solution)/shard_map/all_to_all | solution.py:146
  182.8 9.8 %reshape_reshape.3 = bf16[8,2048,2,1,88]{1,0,4,2,3:T(8,128)(2,1)} reshape(bf16[64,1,256,2,1,88]{2,0,5,3,4,1:T(8,128)(2,1)} %copy.38) | data formatting | bytes 11534336 | tf_op jit(solution)/shard_map/reshape;reshape | solution.py:155
  192.6 8.3 %copy.39 = bf16[8,2048,2,1,88]{1,4,2,3,0:T(8,128)(2,1)} copy(bf16[8,2048,2,1,88]{1,0,4,2,3:T(8,128)(2,1)} %reshape_reshape.3) | data formatting | bytes 11534336
  200.9 76.3 %while.4 = (s32[]{:T(128)}, f32[256,1,8,88]{0,3,2,1:T(8,128)S(1)}, f32[256,1,8]{0,2,1:T(8,128)S(1)}, bf16[8,2048,2,1,88]{1,4,2,3,0:T(8,128)(2,1)}, s32[8,2048]{1...) while((s32[]{:T(128)}, f32[256,1,8,88]{0,3,2,1:T(8,128)S(1)}, ...), condition=%wide.region_17.18_spmd.clone, body=%wide.region_15.17_spmd.clone.sunk | while | flops 1503496704 | bytes 39177352 | solution.py:178
  203.5 3.9 %fusion.81 = (f32[256,8]{0,1:T(8,128)S(1)}, f32[2048,256,8]{1,0,2:T(8,128)S(1)}) fusion(pred[256,2048]{0,1:T(8,128)(4,1)S(1)} %compare_and_fusion.2, bf16[256,1,8,88]{0,3,2,1:T(8,128)(2,1)S(1)} %get-tuple-element.276, bf16[2048,2,1,88]{0,3,2,1:T(8,128)(2,1)S(1)} %dynamic-slice_bitcast_fusion.2), kind=kOutput, calls=%fused_computation.4.clone.1 | convolution fusion | flops 750778368 | bytes 18030592 | tf_op jit(solution)/shard_map/while/body/eval_jaxpr/qkgd,lkd->qkgl/dot_general | solution.py:160
  207.4 2.9 fusion.82
  213.1 3.9 %fusion.81 = (f32[256,8]{0,1:T(8,128)S(1)}, f32[2048,256,8]{1,0,2:T(8,128)S(1)}) fusion(pred[256,2048]{0,1:T(8,128)(4,1)S(1)} %compare_and_fusion.2, bf16[256,1,8,88]{0,3,2,1:T(8,128)(2,1)S(1)} %get-tuple-element.276, bf16[2048,2,1,88]{0,3,2,1:T(8,128)(2,1)S(1)} %dynamic-slice_bitcast_fusion.2), kind=kOutput, calls=%fused_computation.4.clone.1 | convolution fusion | flops 750778368 | bytes 18030592 | tf_op jit(solution)/shard_map/while/body/eval_jaxpr/qkgd,lkd->qkgl/dot_general | solution.py:160
  217.0 2.9 fusion.82
  222.6 3.9 %fusion.81 = (f32[256,8]{0,1:T(8,128)S(1)}, f32[2048,256,8]{1,0,2:T(8,128)S(1)}) fusion(pred[256,2048]{0,1:T(8,128)(4,1)S(1)} %compare_and_fusion.2, bf16[256,1,8,88]{0,3,2,1:T(8,128)(2,1)S(1)} %get-tuple-element.276, bf16[2048,2,1,88]{0,3,2,1:T(8,128)(2,1)S(1)} %dynamic-slice_bitcast_fusion.2), kind=kOutput, calls=%fused_computation.4.clone.1 | convolution fusion | flops 750778368 | bytes 18030592 | tf_op jit(solution)/shard_map/while/body/eval_jaxpr/qkgd,lkd->qkgl/dot_general | solution.py:160
  226.5 2.9 fusion.82
  232.1 3.9 %fusion.81 = (f32[256,8]{0,1:T(8,128)S(1)}, f32[2048,256,8]{1,0,2:T(8,128)S(1)}) fusion(pred[256,2048]{0,1:T(8,128)(4,1)S(1)} %compare_and_fusion.2, bf16[256,1,8,88]{0,3,2,1:T(8,128)(2,1)S(1)} %get-tuple-element.276, bf16[2048,2,1,88]{0,3,2,1:T(8,128)(2,1)S(1)} %dynamic-slice_bitcast_fusion.2), kind=kOutput, calls=%fused_computation.4.clone.1 | convolution fusion | flops 750778368 | bytes 18030592 | tf_op jit(solution)/shard_map/while/body/eval_jaxpr/qkgd,lkd->qkgl/dot_general | solution.py:160
  236.1 2.9 fusion.82
  241.7 3.9 %fusion.81 = (f32[256,8]{0,1:T(8,128)S(1)}, f32[2048,256,8]{1,0,2:T(8,128)S(1)}) fusion(pred[256,2048]{0,1:T(8,128)(4,1)S(1)} %compare_and_fusion.2, bf16[256,1,8,88]{0,3,2,1:T(8,128)(2,1)S(1)} %get-tuple-element.276, bf16[2048,2,1,88]{0,3,2,1:T(8,128)(2,1)S(1)} %dynamic-slice_bitcast_fusion.2), kind=kOutput, calls=%fused_computation.4.clone.1 | convolution fusion | flops 750778368 | bytes 18030592 | tf_op jit(solution)/shard_map/while/body/eval_jaxpr/qkgd,lkd->qkgl/dot_general | solution.py:160
  245.6 2.9 fusion.82
  251.2 3.9 %fusion.81 = (f32[256,8]{0,1:T(8,128)S(1)}, f32[2048,256,8]{1,0,2:T(8,128)S(1)}) fusion(pred[256,2048]{0,1:T(8,128)(4,1)S(1)} %compare_and_fusion.2, bf16[256,1,8,88]{0,3,2,1:T(8,128)(2,1)S(1)} %get-tuple-element.276, bf16[2048,2,1,88]{0,3,2,1:T(8,128)(2,1)S(1)} %dynamic-slice_bitcast_fusion.2), kind=kOutput, calls=%fused_computation.4.clone.1 | convolution fusion | flops 750778368 | bytes 18030592 | tf_op jit(solution)/shard_map/while/body/eval_jaxpr/qkgd,lkd->qkgl/dot_general | solution.py:160
  255.2 2.9 fusion.82
  260.8 3.9 %fusion.81 = (f32[256,8]{0,1:T(8,128)S(1)}, f32[2048,256,8]{1,0,2:T(8,128)S(1)}) fusion(pred[256,2048]{0,1:T(8,128)(4,1)S(1)} %compare_and_fusion.2, bf16[256,1,8,88]{0,3,2,1:T(8,128)(2,1)S(1)} %get-tuple-element.276, bf16[2048,2,1,88]{0,3,2,1:T(8,128)(2,1)S(1)} %dynamic-slice_bitcast_fusion.2), kind=kOutput, calls=%fused_computation.4.clone.1 | convolution fusion | flops 750778368 | bytes 18030592 | tf_op jit(solution)/shard_map/while/body/eval_jaxpr/qkgd,lkd->qkgl/dot_general | solution.py:160
  264.7 2.9 fusion.82
  270.3 3.9 %fusion.81 = (f32[256,8]{0,1:T(8,128)S(1)}, f32[2048,256,8]{1,0,2:T(8,128)S(1)}) fusion(pred[256,2048]{0,1:T(8,128)(4,1)S(1)} %compare_and_fusion.2, bf16[256,1,8,88]{0,3,2,1:T(8,128)(2,1)S(1)} %get-tuple-element.276, bf16[2048,2,1,88]{0,3,2,1:T(8,128)(2,1)S(1)} %dynamic-slice_bitcast_fusion.2), kind=kOutput, calls=%fused_computation.4.clone.1 | convolution fusion | flops 750778368 | bytes 18030592 | tf_op jit(solution)/shard_map/while/body/eval_jaxpr/qkgd,lkd->qkgl/dot_general | solution.py:160
  274.3 2.9 fusion.82
  277.3 3.6 %fusion.68 = f32[256,1408]{1,0:T(8,128)} fusion(bf16[256,704]{0,1:T(8,128)(2,1)S(1)} %bitcast.200, bf16[704,1408]{1,0:T(8,128)(2,1)} %param.25), kind=kOutput, calls=%fused_computation.147 | convolution fusion | flops 507510784 | bytes 3784704 | tf_op jit(solution)/shard_map/dot_general | solution.py:183
  280.9 27.8 %all-reduce.6.cloned.1.call-done = f32[256,1408]{1,0:T(8,128)} async-done(((f32[256,1408]{1,0:T(8,128)}), f32[256,1408]{1,0:T(8,128)}) %all-reduce.6.cloned.1.call-update) | async-done | bytes 1441808 | tf_op jit(solution)/shard_map/psum | solution.py:184
  (119 shorter events, 43.9 us)
Async XLA Ops:
  6.5 14.2 %copy-start = (bf16[704,1408]{1,0:T(8,128)(2,1)S(1)}, bf16[704,1408]{1,0:T(8,128)(2,1)}, u32[]{:S(2)}) copy-start(bf16[704,1408]{1,0:T(8,128)(2,1)} %param.21) | copy-start | bytes 5947396
  6.5 2.6 copy-start.3
  6.5 49.3 %all-reduce.4.cloned.1.call-start = ((), (), s32[]{:S(2)}) async-start(), calls=%async_computation.2 | async-start | bytes 5767168 | tf_op jit(solution)/shard_map/psum | solution.py:100
  20.7 3.1 copy-start.5
  23.8 2.6 copy-start.6
  64.0 28.6 %copy-start.2 = (bf16[256,1,1408]{2,0,1:T(8,128)(2,1)S(1)}, bf16[256,1,1408]{2,0,1:T(8,128)(2,1)}, u32[]{:S(2)}) copy-start(bf16[256,1,1408]{2,0,1:T(8,128)(2,1)} %param.18) | copy-start | bytes 2162692
  71.8 20.8 %all-to-all-start = ((bf16[2,64,1408]{2,0,1:T(2,128)(2,1)}), bf16[2,64,1408]{2,0,1:T(2,128)(2,1)S(1)}, u32[]{:S(2)}, u32[]{:S(2)}) async-start(bf16[2,64,1408]{2,0,1:T(2,128)(2,1)} %fusion.51), calls=%async_computation | async-start | bytes 720896 | tf_op jit(solution)/shard_map/all_to_all | solution.py:111
  92.6 1.8 copy-start.7
  98.0 5.9 %copy-start.4 = (s32[256,64]{0,1:T(8,128)S(1)}, s32[256,64]{0,1:T(8,128)}, u32[]{:S(2)}) copy-start(s32[256,64]{0,1:T(8,128)} %param.19) | copy-start | bytes 196612
  98.0 77.6 %all-to-all-start.1 = ((bf16[64,1,256,2,1,88]{2,5,3,4,1,0:T(8,128)(2,1)}), bf16[64,1,256,2,1,88]{2,5,3,4,1,0:T(8,128)(2,1)}, u32[]{:S(2)}, u32[]{:S(2)}) async-start(bf16[64,1,256,2,1,88]{2,5,3,4,1,0:T(8,128)(2,1)} %stack.20), calls=%async_computation.1 | async-start | bytes 11534336 | tf_op jit(solution)/shard_map/all_to_all | solution.py:146
  103.8 204.9 %all-reduce.6.cloned.1.call-start = ((), (), s32[]{:S(2)}) async-start(), calls=%async_computation.3 | async-start | bytes 2883584 | tf_op jit(solution)/shard_map/psum | solution.py:184
  277.3 33.8 %copy-start.1 = (bf16[704,1408]{1,0:T(8,128)(2,1)S(1)}, bf16[704,1408]{1,0:T(8,128)(2,1)}, u32[]{:S(2)}) copy-start(bf16[704,1408]{1,0:T(8,128)(2,1)} %param.21) | copy-start | bytes 5947396
Sparse Core Ops, SparseCore 0:
  23.9 31.8 all-reduce.3
  281.1 27.6 all-reduce.5
